TPU v7x, 128 devices: a whole 4x4x4 slice. The times are simulated.
128 devices in a mesh: row: 8 (over z, core), col: 16 (over y, x).
Axes of the slice: x: 4, y: 4, z: 4, core: 2. Of those that a mesh axis runs over, the one named last changes fastest.
Arguments:
- psi_val: float32 [64, 128, 128, 128], P(None, 'row', 'col'), may hold values from -6 to 6
- psi_cond: float32 [64, 128, 128, 128], P(None, 'row', 'col'), may hold values from -6 to 6
- eps_val: float32 [64], replicated, may hold values from -12 to -1
- eps_cond: float32 [64], replicated, may hold values from 1 to 12
- val_index: int32 [128], replicated, may hold values from 0 to 63
- cond_index: int32 [128], replicated, may hold values from 0 to 63
- gmap: int32 [8192], replicated, may hold values from 0 to 2097151, as said below
- chi0_in: float32 [2, 8192, 8192], P(None, 'row', 'col'), may hold values from -6 to 6
Outputs:
- chi0_out: float32 [2, 8192, 8192], P(None, 'row', 'col')
Inputs may be any that keep to these rules, and one draw needn't show every extreme that they name: gmap holds 8192 distinct entries. Entries g of device block d = g // 64 (d = r * 16 + c) have ky in [r * 16, (r + 1) * 16) and kz in [c * 8, (c + 1) * 8); kx is any.
All inputs are finite; a program needn't handle non-finite values.
Results may differ from a plain program's by a relative error of at most 0.000068.
Values sent between devices are 32-bit elements; how exact they have to be, the bound alone decides.
No kernel may reach another device: no remote copies, remote signals or barrier semaphores. Data moves between devices by JAX's collectives and lax.ppermute only.
A program may use at most 128 MiB of HBM per device.

v0:
```python
import math
import jax
import jax.numpy as jnp
from jax import lax
from jax.sharding import PartitionSpec as P

GRID = 128
NG = 8192
HIGH = lax.Precision.HIGHEST


def spread(block, axis, holder):
    block = jnp.where(lax.axis_index(axis) == holder, block, jnp.zeros_like(block))
    return lax.psum(block, axis)


def dft_tables(length):
    steps = jnp.arange(length, dtype=jnp.int32)
    phase = steps[:, None] * steps[None, :] % length
    angle = phase.astype(jnp.float32) * (2.0 * math.pi / length)
    return (jnp.cos(angle), jnp.sin(angle))


def point_tables(freq_x, length):
    steps = jnp.arange(length, dtype=jnp.int32)
    phase = steps[:, None] * freq_x[None, :] % length
    angle = phase.astype(jnp.float32) * (2.0 * math.pi / length)
    return (jnp.cos(angle), jnp.sin(angle))


def pick_points(real_part, imag_part, yz_index, cos_x, sin_x):
    count = real_part.shape[0]
    flat_re = real_part.reshape(count, real_part.shape[1], -1)
    flat_im = imag_part.reshape(count, imag_part.shape[1], -1)
    cols_re = jnp.take(flat_re, yz_index, axis=2)
    cols_im = jnp.take(flat_im, yz_index, axis=2)
    m_re = jnp.sum(cols_re * cos_x[None] + cols_im * sin_x[None], axis=1)
    m_im = jnp.sum(cols_im * cos_x[None] - cols_re * sin_x[None], axis=1)
    return (m_re, m_im)


def contract_pairs(left, right):
    return lax.dot_general(
        left, right, (((0,), (0,)), ((), ())), precision=HIGH, preferred_element_type=jnp.float32
    )


def on_device(psi_val, psi_cond, eps_val, eps_cond, val_index, cond_index, gmap, chi0_in):
    pairs = val_index.shape[0]
    scale = 1.0 / math.sqrt(GRID**3)
    cos_t, sin_t = dft_tables(GRID)
    rho = jnp.take(psi_val, val_index, axis=0) * jnp.take(psi_cond, cond_index, axis=0)
    row_pos = lax.axis_index("row")
    col_pos = lax.axis_index("col")
    mesh_cols = lax.axis_size("col")
    mesh_rows = lax.axis_size("row")
    per_device = NG // (mesh_rows * mesh_cols)
    row_span = GRID // mesh_rows
    col_span = GRID // mesh_cols
    flat_pos = row_pos * mesh_cols + col_pos
    own_map = lax.dynamic_slice_in_dim(gmap, flat_pos * per_device, per_device, 0)
    freq_x = own_map // (GRID * GRID)
    freq_y = own_map // GRID % GRID - row_pos * row_span
    freq_z = own_map % GRID - col_pos * col_span
    yz_index = freq_y * col_span + freq_z
    cos_x, sin_x = point_tables(freq_x, GRID)
    z_re = jnp.einsum("pxyz,zk->pxyk", rho, cos_t, precision=HIGH)
    z_im = -jnp.einsum("pxyz,zk->pxyk", rho, sin_t, precision=HIGH)
    part_re = lax.all_to_all(z_re, "col", split_axis=3, concat_axis=2, tiled=True)
    part_im = lax.all_to_all(z_im, "col", split_axis=3, concat_axis=2, tiled=True)
    y_re = jnp.einsum("pxyz,yk->pxkz", part_re, cos_t, precision=HIGH) + jnp.einsum(
        "pxyz,yk->pxkz", part_im, sin_t, precision=HIGH
    )
    y_im = jnp.einsum("pxyz,yk->pxkz", part_im, cos_t, precision=HIGH) - jnp.einsum(
        "pxyz,yk->pxkz", part_re, sin_t, precision=HIGH
    )
    y_re, y_im = (y_re, y_im)
    m_re, m_im = pick_points(
        lax.all_to_all(y_re, "row", split_axis=2, concat_axis=1, tiled=True),
        lax.all_to_all(y_im, "row", split_axis=2, concat_axis=1, tiled=True),
        yz_index,
        cos_x,
        sin_x,
    )
    m_re = m_re * scale
    m_im = m_im * scale
    cols_span = chi0_in.shape[2]
    rows_re, rows_im = (
        lax.all_gather(m_re, "col", axis=1, tiled=True),
        lax.all_gather(m_im, "col", axis=1, tiled=True),
    )
    offset = col_pos * mesh_rows % mesh_cols * per_device
    piece_re = lax.dynamic_slice_in_dim(rows_re, offset, cols_span, 1)
    piece_im = lax.dynamic_slice_in_dim(rows_im, offset, cols_span, 1)
    root = col_pos * mesh_rows // mesh_cols
    cols_re, cols_im = (spread(piece_re, "row", root), spread(piece_im, "row", root))
    val_hot = val_index[:, None] == jnp.arange(eps_val.shape[0], dtype=jnp.int32)[None, :]
    cond_hot = cond_index[:, None] == jnp.arange(eps_cond.shape[0], dtype=jnp.int32)[None, :]
    energy_v = jnp.sum(jnp.where(val_hot, eps_val[None, :], 0.0), axis=1)
    energy_c = jnp.sum(jnp.where(cond_hot, eps_cond[None, :], 0.0), axis=1)
    weight = (-6.0 / (math.sqrt(pairs) * (energy_c - energy_v)))[:, None]
    out_re = (
        chi0_in[0]
        + contract_pairs(weight * rows_re, cols_re)
        + contract_pairs(weight * rows_im, cols_im)
    )
    out_im = (
        chi0_in[1]
        + contract_pairs(weight * rows_im, cols_re)
        - contract_pairs(weight * rows_re, cols_im)
    )
    return jnp.stack([out_re, out_im])


def solution(mesh):
    return jax.shard_map(
        on_device,
        mesh=mesh,
        in_specs=(
            P(None, "row", "col", None),
            P(None, "row", "col", None),
            P(),
            P(),
            P(),
            P(),
            P(),
            P(None, "row", "col"),
        ),
        out_specs=P(None, "row", "col"),
        check_vma=False,
    )
```

profile of v0, /device:TPU:0, one launch (start us, length us, event | category | flops | bytes accessed | tf_op | source)
XLA Modules:
  0.0 716.1 jit_solution(10853611819511883215)
XLA Ops:
  6.5 0.7 compare_select_fusion.1
  7.2 0.7 compare_and_fusion.1
  7.9 6.5 gather_fusion.1
  14.4 6.5 gather_fusion
  20.9 6.5 select_multiply_fusion
  27.4 3.2 copy-done
  30.7 14.7 %fusion.6 = f32[128,16,8,128]{3,0,2,1:T(8,128)} fusion(f32[128,16,8,128]{3,2,1,0:T(8,128)S(1)} %select_multiply_fusion), kind=kOutput, calls=%fused_computation.18 | convolution fusion | flops 3223552000 | bytes 16777216 | tf_op jit(solution)/shard_map/pxyz,zk->pxyk/dot_general | solution.py:68
  45.4 9.3 %copy.79 = f32[128,16,8,128]{0,2,1,3:T(8,128)} copy(f32[128,16,8,128]{3,0,2,1:T(8,128)} %fusion.6) | data formatting | bytes 16777216 | tf_op jit(solution)/shard_map/neg | solution.py:68
  54.7 7.4 %all-to-all-start.1 = ((f32[128,16,8,128]{0,2,1,3:T(8,128)}), f32[128,16,8,128]{0,2,1,3:T(8,128)}, u32[]{:S(2)}, u32[]{:S(2)}) async-start(f32[128,16,8,128]{0,2,1,3:T(8,128)} %copy.79), calls=%async_computation.1 | async-start | bytes 16777216 | tf_op jit(solution)/shard_map/all_to_all | solution.py:70
  62.1 11.3 %fusion.29 = f32[128,16,8,128]{3,2,1,0:T(8,128)} fusion(f32[128,16,8,128]{3,2,1,0:T(8,128)} %copy-done), kind=kOutput, calls=%fused_computation.46 | convolution fusion | flops 3221454848 | bytes 16777216 | tf_op jit(solution)/shard_map/pxyz,zk->pxyk/dot_general | solution.py:67
  73.4 9.3 %copy.73 = f32[128,16,8,128]{0,2,1,3:T(8,128)} copy(f32[128,16,8,128]{3,2,1,0:T(8,128)} %fusion.29) | data formatting | bytes 16777216 | tf_op jit(solution)/shard_map/pxyz,zk->pxyk/dot_general | solution.py:67
  82.7 103.4 %all-to-all-done.1 = f32[128,16,8,128]{0,2,1,3:T(8,128)} async-done(((f32[128,16,8,128]{0,2,1,3:T(8,128)}), f32[128,16,8,128]{0,2,1,3:T(8,128)}, u32[]{:S(2)}, u32[]{:S(2)}) %all-to-all-start.1) | async-done | bytes 8388640 | tf_op jit(solution)/shard_map/all_to_all | solution.py:70
  186.1 5.7 all-to-all-start
  191.9 11.5 %copy.81 = f32[128,16,16,8,8]{0,4,3,2,1:T(8,128)} copy(f32[128,16,16,8,8]{0,3,1,4,2:T(8,128)} %bitcast.13) | data formatting | bytes 16777216 | tf_op jit(solution)/shard_map/all_to_all | solution.py:70
  203.3 9.3 %copy.82 = f32[128,16,128,8]{2,0,3,1:T(8,128)} copy(f32[128,16,128,8]{0,3,2,1:T(8,128)} %bitcast.83) | data formatting | bytes 16777216 | tf_op jit(solution)/shard_map/all_to_all | solution.py:70
  212.6 12.3 %fusion.31 = f32[128,128,16,8]{1,0,3,2:T(8,128)} fusion(f32[128,16,128,8]{2,0,3,1:T(8,128)} %copy.82), kind=kOutput, calls=%fused_computation.48 | convolution fusion | flops 3221454848 | bytes 16777216 | tf_op jit(solution)/shard_map/pxyz,yk->pxkz/dot_general | solution.py:74
  224.9 88.9 %all-to-all-done = f32[128,16,8,128]{0,2,1,3:T(8,128)} async-done(((f32[128,16,8,128]{0,2,1,3:T(8,128)}), f32[128,16,8,128]{0,2,1,3:T(8,128)}, u32[]{:S(2)}, u32[]{:S(2)}) %all-to-all-start) | async-done | bytes 8388640 | tf_op jit(solution)/shard_map/all_to_all | solution.py:69
  313.8 11.5 %copy.75 = f32[128,16,16,8,8]{0,4,3,2,1:T(8,128)} copy(f32[128,16,16,8,8]{0,3,1,4,2:T(8,128)} %bitcast.6) | data formatting | bytes 16777216 | tf_op jit(solution)/shard_map/all_to_all | solution.py:69
  325.3 9.3 %copy.76 = f32[128,16,128,8]{2,0,3,1:T(8,128)} copy(f32[128,16,128,8]{0,3,2,1:T(8,128)} %bitcast.84) | data formatting | bytes 16777216 | tf_op jit(solution)/shard_map/all_to_all | solution.py:69
  334.5 12.4 %subtract_bitcast_fusion = f32[128,16,128,8]{0,2,3,1:T(8,128)S(1)} fusion(f32[128,128,16,8]{1,0,3,2:T(8,128)} %fusion.31, f32[128,16,128,8]{2,0,3,1:T(8,128)} %copy.76), kind=kOutput, calls=%fused_computation.7 | convolution fusion | flops 3223552000 | bytes 25165824 | tf_op jit(solution)/shard_map/pxyz,yk->pxkz/dot_general | solution.py:74
  347.0 8.1 %copy.89 = f32[128,16,128,8]{0,3,1,2:T(8,128)} copy(f32[128,16,128,8]{0,2,3,1:T(8,128)S(1)} %subtract_bitcast_fusion) | data formatting | bytes 16777216 | tf_op jit(solution)/shard_map/sub | solution.py:74
  355.0 5.6 all-to-all-start.3
  360.6 10.0 %fusion.33 = f32[128,128,16,8]{1,0,3,2:T(8,128)S(1)} fusion(f32[128,16,128,8]{2,0,3,1:T(8,128)} %copy.76), kind=kOutput, calls=%fused_computation.50 | convolution fusion | flops 3221454848 | bytes 16777216 | tf_op jit(solution)/shard_map/pxyz,yk->pxkz/dot_general | solution.py:71
  370.6 10.3 %add_bitcast_fusion = f32[128,16,128,8]{0,2,3,1:T(8,128)S(1)} fusion(f32[128,128,16,8]{1,0,3,2:T(8,128)S(1)} %fusion.33, f32[128,16,128,8]{2,0,3,1:T(8,128)} %copy.82), kind=kOutput, calls=%fused_computation.8 | convolution fusion | flops 3223552000 | bytes 25165824 | tf_op jit(solution)/shard_map/pxyz,yk->pxkz/dot_general | solution.py:71
  380.9 8.1 %copy.83 = f32[128,16,128,8]{0,3,1,2:T(8,128)} copy(f32[128,16,128,8]{0,2,3,1:T(8,128)S(1)} %add_bitcast_fusion) | data formatting | bytes 16777216 | tf_op jit(solution)/shard_map/add | solution.py:71
  389.0 66.3 %all-to-all-done.3 = f32[128,16,128,8]{0,3,1,2:T(8,128)} async-done(((f32[128,16,128,8]{0,3,1,2:T(8,128)}), f32[128,16,128,8]{0,3,1,2:T(8,128)}, u32[]{:S(2)}, u32[]{:S(2)}) %all-to-all-start.3) | async-done | bytes 8388640 | tf_op jit(solution)/shard_map/all_to_all | solution.py:80
  455.3 4.9 all-to-all-start.2
  460.3 0.8 and_select_fusion
  461.1 0.8 compare_and_fusion
  461.9 0.2 fusion.53
  462.1 7.8 %copy.91 = f32[128,8,16,16,8]{0,4,3,2,1:T(8,128)} copy(f32[128,8,16,16,8]{0,4,2,3,1:T(8,128)} %bitcast.26) | data formatting | bytes 16777216 | tf_op jit(solution)/shard_map/all_to_all | solution.py:80
  469.9 9.3 %copy.92 = f32[128,128,128]{1,0,2:T(8,128)} copy(f32[128,128,128]{0,2,1:T(8,128)} %bitcast.85) | data formatting | bytes 16777216 | tf_op jit(solution)/shard_map/reshape | solution.py:34
  479.2 75.7 %all-to-all-done.2 = f32[128,16,128,8]{0,3,1,2:T(8,128)} async-done(((f32[128,16,128,8]{0,3,1,2:T(8,128)}), f32[128,16,128,8]{0,3,1,2:T(8,128)}, u32[]{:S(2)}, u32[]{:S(2)}) %all-to-all-start.2) | async-done | bytes 8388640 | tf_op jit(solution)/shard_map/all_to_all | solution.py:79
  554.8 7.8 %copy.85 = f32[128,8,16,16,8]{0,4,3,2,1:T(8,128)} copy(f32[128,8,16,16,8]{0,4,2,3,1:T(8,128)} %bitcast.18) | data formatting | bytes 16777216 | tf_op jit(solution)/shard_map/all_to_all | solution.py:79
  562.6 9.3 %copy.86 = f32[128,128,128]{1,0,2:T(8,128)} copy(f32[128,128,128]{0,2,1:T(8,128)} %bitcast.86) | data formatting | bytes 16777216 | tf_op jit(solution)/shard_map/reshape | solution.py:33
  571.9 6.2 gather_fusion.3
  578.1 6.2 gather_fusion.2
  584.3 4.9 fusion.5
  589.3 23.2 %all_gather.6 = f32[128,1024]{0,1:T(8,128)S(1)} all-gather(f32[128,64]{0,1:T(8,128)S(1)} %broadcast_multiply_fusion.1), channel_id=1, replica_groups=mesh['row'=8,'col'=16] {'col'}, dimensions={1}, use_global_device_ids=true | all-gather | bytes 557056 | tf_op jit(solution)/shard_map/all_gather | solution.py:89
  612.5 22.3 %all_gather.7 = f32[128,1024]{0,1:T(8,128)S(1)} all-gather(f32[128,64]{0,1:T(8,128)S(1)} %broadcast_multiply_fusion), channel_id=1, replica_groups=mesh['row'=8,'col'=16] {'col'}, dimensions={1}, use_global_device_ids=true | all-gather | bytes 557056 | tf_op jit(solution)/shard_map/all_gather | solution.py:90
  634.8 0.7 dynamic-slice_select_fusion.1
  635.5 0.7 dynamic-slice_select_fusion
  636.4 58.5 %all-reduce.3.cloned.1.call-done = (f32[128,512]{0,1:T(8,128)}, f32[128,512]{0,1:T(8,128)}) async-done(((f32[128,512]{0,1:T(8,128)}, f32[128,512]{0,1:T(8,128)}), (f32[128,512]{0,1:T(8,128)}, f32[128,512]{0,1:T(8,128)})) %all-reduce.3.cloned.1.call-update) | async-done | bytes 524304 | tf_op jit(solution)/shard_map/psum | solution.py:14
  694.9 2.9 fusion.13
  697.8 2.7 fusion.17
  700.6 3.7 fusion.10
  704.3 2.0 fusion.12
  706.3 2.5 pad_maximum_fusion
  (22 shorter events, 0.2 us)
Async XLA Ops:
  27.4 3.2 copy-start
  54.7 131.5 %all-to-all-start.1 = ((f32[128,16,8,128]{0,2,1,3:T(8,128)}), f32[128,16,8,128]{0,2,1,3:T(8,128)}, u32[]{:S(2)}, u32[]{:S(2)}) async-start(f32[128,16,8,128]{0,2,1,3:T(8,128)} %copy.79), calls=%async_computation.1 | async-start | bytes 16777216 | tf_op jit(solution)/shard_map/all_to_all | solution.py:70
  186.1 127.6 %all-to-all-start = ((f32[128,16,8,128]{0,2,1,3:T(8,128)}), f32[128,16,8,128]{0,2,1,3:T(8,128)}, u32[]{:S(2)}, u32[]{:S(2)}) async-start(f32[128,16,8,128]{0,2,1,3:T(8,128)} %copy.73), calls=%async_computation | async-start | bytes 16777216 | tf_op jit(solution)/shard_map/all_to_all | solution.py:69
  355.0 100.2 %all-to-all-start.3 = ((f32[128,16,128,8]{0,3,1,2:T(8,128)}), f32[128,16,128,8]{0,3,1,2:T(8,128)}, u32[]{:S(2)}, u32[]{:S(2)}) async-start(f32[128,16,128,8]{0,3,1,2:T(8,128)} %copy.89), calls=%async_computation.3 | async-start | bytes 16777216 | tf_op jit(solution)/shard_map/all_to_all | solution.py:80
  455.3 99.6 %all-to-all-start.2 = ((f32[128,16,128,8]{0,3,1,2:T(8,128)}), f32[128,16,128,8]{0,3,1,2:T(8,128)}, u32[]{:S(2)}, u32[]{:S(2)}) async-start(f32[128,16,128,8]{0,3,1,2:T(8,128)} %copy.83), calls=%async_computation.2 | async-start | bytes 16777216 | tf_op jit(solution)/shard_map/all_to_all | solution.py:79
  460.2 234.7 %all-reduce.3.cloned.1.call-start = ((), (), s32[]{:S(2)}) async-start(), calls=%async_computation.4 | async-start | bytes 1048576 | tf_op jit(solution)/shard_map/psum | solution.py:14
  584.3 51.9 %copy-start.3 = (s32[128]{0:T(128)S(1)}, s32[128]{0:T(128)}, u32[]{:S(2)}) copy-start(s32[128]{0:T(128)} %param.17) | copy-start | bytes 1540
  584.3 52.0 %copy-start.4 = (s32[128]{0:T(128)S(1)}, s32[128]{0:T(128)}, u32[]{:S(2)}) copy-start(s32[128]{0:T(128)} %param.16) | copy-start | bytes 1540
  584.3 52.0 %copy-start.5 = (f32[64]{0:T(128)S(1)}, f32[64]{0:T(128)}, u32[]{:S(2)}) copy-start(f32[64]{0:T(128)} %param.14) | copy-start | bytes 772
  584.3 52.0 %copy-start.6 = (f32[64]{0:T(128)S(1)}, f32[64]{0:T(128)}, u32[]{:S(2)}) copy-start(f32[64]{0:T(128)} %param.15) | copy-start | bytes 772
  694.9 9.4 %copy-start.1 = (f32[2,1024,512]{2,1,0:T(8,128)S(1)}, f32[2,1024,512]{2,1,0:T(8,128)}, u32[]{:S(2)}) copy-start(f32[2,1024,512]{2,1,0:T(8,128)} %param.19) | copy-start | bytes 12582916
  694.9 9.4 %copy-start.2 = (f32[128,512]{0,1:T(8,128)S(1)}, f32[128,512]{0,1:T(8,128)}, u32[]{:S(2)}) copy-start(f32[128,512]{0,1:T(8,128)} %get-tuple-element.10) | copy-start | bytes 786436
Sparse Core Ops, SparseCore 0:
  636.4 58.4 all-reduce.2
where the time goes:
time: 724 us; the launch traced here: 716 us
  waiting for transfers between devices  393 us (54%)
  local copies, waits for them, and re-layouts  139 us (19%)
  matrix products  82.4 us (11%)
  blocking collectives  45.5 us (6%)
  starting transfers between devices  23.7 us (3%)
  other arithmetic  18.6 us (3%)
  between operations  14.2 us (2%)
    all_to_all x1, waiting for transfers between devices, on_device(): lax.all_to_all(z_im, 'col', split_axis=3, concat_axis=2, tiled=True)  103 us
    all_to_all x1, waiting for transfers between devices, on_device(): lax.all_to_all(z_re, 'col', split_axis=3, concat_axis=2, tiled=True)  88.9 us
    all_to_all x1, waiting for transfers between devices, on_device(): lax.all_to_all(y_re, 'row', split_axis=2, concat_axis=1, tiled=True)  75.7 us
    all_to_all x1, waiting for transfers between devices, on_device(): lax.all_to_all(y_im, 'row', split_axis=2, concat_axis=1, tiled=True)  66.3 us
    psum x1, waiting for transfers between devices, spread(): return lax.psum(block, axis)  58.5 us
    all_gather x1, blocking collectives, on_device(): lax.all_gather(m_re, 'col', axis=1, tiled=True)  23.2 us
    all_gather x1, blocking collectives, on_device(): lax.all_gather(m_im, 'col', axis=1, tiled=True)  22.3 us
    all_to_all x2, local copies, waits for them, and re-layouts, on_device(): lax.all_to_all(z_re, 'col', split_axis=3, concat_axis=2, tiled=True)  20.7 us
  transfers between devices with their start and end apart: 5, of which 5 were waited for; matrix products, arithmetic and copies ran while one was open for 14% of the time, Pallas kernels for 0%

commit v1 on v0

--- a/solution.py
+++ b/solution.py
@@ -11,7 +11,7 @@
 
 def spread(block, axis, holder):
     block = jnp.where(lax.axis_index(axis) == holder, block, jnp.zeros_like(block))
-    return lax.psum(block, axis)
+    return jnp.sum(lax.all_gather(block, axis), 0)
 
 
 def dft_tables(length):

time: 724 us -> 696 us (0.961)
  waiting for transfers between devices: 393 us -> 358 us
    psum x1 -> x0, waiting for transfers between devices: 58.5 us -> none  [spread(): return lax.psum(block, axis)]
    all_gather x0 -> x2, waiting for transfers between devices: none -> 23.6 us  [spread(): return jnp.sum(lax.all_gather(block, axis), 0)]
  transfers between devices with their start and end apart: 5 -> 6, of which waited for: 5 -> 6; matrix products, arithmetic and copies ran while one was open for 14% -> 16% of each run, Pallas kernels for 0% -> 0%
where the time goes in v1:
time: 696 us; the launch traced here: 686 us
  waiting for transfers between devices  358 us (51%)
  local copies, waits for them, and re-layouts  144 us (21%)
  matrix products  82.2 us (12%)
  blocking collectives  45.4 us (7%)
  starting transfers between devices  23.7 us (3%)
  other arithmetic  19.6 us (3%)
  between operations  14.2 us (2%)
    all_to_all x1, waiting for transfers between devices, on_device(): lax.all_to_all(z_im, 'col', split_axis=3, concat_axis=2, tiled=True)  103 us
    all_to_all x1, waiting for transfers between devices, on_device(): lax.all_to_all(z_re, 'col', split_axis=3, concat_axis=2, tiled=True)  88.9 us
    all_to_all x1, waiting for transfers between devices, on_device(): lax.all_to_all(y_re, 'row', split_axis=2, concat_axis=1, tiled=True)  75.7 us
    all_to_all x1, waiting for transfers between devices, on_device(): lax.all_to_all(y_im, 'row', split_axis=2, concat_axis=1, tiled=True)  66.2 us
    all_gather x2, waiting for transfers between devices, spread(): return jnp.sum(lax.all_gather(block, axis), 0)  23.6 us
    all_gather x1, blocking collectives, on_device(): lax.all_gather(m_re, 'col', axis=1, tiled=True)  23.1 us
    all_gather x1, blocking collectives, on_device(): lax.all_gather(m_im, 'col', axis=1, tiled=True)  22.3 us
    all_to_all x2, local copies, waits for them, and re-layouts, on_device(): lax.all_to_all(z_re, 'col', split_axis=3, concat_axis=2, tiled=True)  20.8 us
  transfers between devices with their start and end apart: 6, of which 6 were waited for; matrix products, arithmetic and copies ran while one was open for 16% of the time, Pallas kernels for 0%

profile of v1, /device:TPU:0, one launch (start us, length us, event | category | flops | bytes accessed | tf_op | source)
XLA Modules:
  0.0 686.4 jit_solution(5161983749927553127)
XLA Ops:
  7.9 6.5 gather_fusion.1
  14.4 6.5 gather_fusion
  20.9 6.5 select_multiply_fusion
  27.5 3.2 copy-done
  30.7 14.8 %fusion.6 = f32[128,16,8,128]{3,0,2,1:T(8,128)} fusion(f32[128,16,8,128]{3,2,1,0:T(8,128)S(1)} %select_multiply_fusion), kind=kOutput, calls=%fused_computation.18 | convolution fusion | flops 3223552000 | bytes 16777216 | tf_op jit(solution)/shard_map/pxyz,zk->pxyk/dot_general | solution.py:68
  45.5 9.4 %copy.101 = f32[128,16,8,128]{0,2,1,3:T(8,128)} copy(f32[128,16,8,128]{3,0,2,1:T(8,128)} %fusion.6) | data formatting | bytes 16777216 | tf_op jit(solution)/shard_map/neg | solution.py:68
  54.9 7.4 %all-to-all-start.1 = ((f32[128,16,8,128]{0,2,1,3:T(8,128)}), f32[128,16,8,128]{0,2,1,3:T(8,128)}, u32[]{:S(2)}, u32[]{:S(2)}) async-start(f32[128,16,8,128]{0,2,1,3:T(8,128)} %copy.101), calls=%async_computation.1 | async-start | bytes 16777216 | tf_op jit(solution)/shard_map/all_to_all | solution.py:70
  62.3 11.3 %fusion.29 = f32[128,16,8,128]{3,2,1,0:T(8,128)} fusion(f32[128,16,8,128]{3,2,1,0:T(8,128)} %copy-done), kind=kOutput, calls=%fused_computation.48 | convolution fusion | flops 3221454848 | bytes 16777216 | tf_op jit(solution)/shard_map/pxyz,zk->pxyk/dot_general | solution.py:67
  73.6 9.4 %copy.95 = f32[128,16,8,128]{0,2,1,3:T(8,128)} copy(f32[128,16,8,128]{3,2,1,0:T(8,128)} %fusion.29) | data formatting | bytes 16777216 | tf_op jit(solution)/shard_map/pxyz,zk->pxyk/dot_general | solution.py:67
  83.0 103.4 %all-to-all-done.1 = f32[128,16,8,128]{0,2,1,3:T(8,128)} async-done(((f32[128,16,8,128]{0,2,1,3:T(8,128)}), f32[128,16,8,128]{0,2,1,3:T(8,128)}, u32[]{:S(2)}, u32[]{:S(2)}) %all-to-all-start.1) | async-done | bytes 8388640 | tf_op jit(solution)/shard_map/all_to_all | solution.py:70
  186.3 5.7 all-to-all-start
  192.1 11.5 %copy.103 = f32[128,16,16,8,8]{0,4,3,2,1:T(8,128)} copy(f32[128,16,16,8,8]{0,3,1,4,2:T(8,128)} %bitcast.13) | data formatting | bytes 16777216 | tf_op jit(solution)/shard_map/all_to_all | solution.py:70
  203.5 9.3 %copy.104 = f32[128,16,128,8]{2,0,3,1:T(8,128)} copy(f32[128,16,128,8]{0,3,2,1:T(8,128)} %bitcast.93) | data formatting | bytes 16777216 | tf_op jit(solution)/shard_map/all_to_all | solution.py:70
  212.8 12.3 %fusion.31 = f32[128,128,16,8]{1,0,3,2:T(8,128)} fusion(f32[128,16,128,8]{2,0,3,1:T(8,128)} %copy.104), kind=kOutput, calls=%fused_computation.50 | convolution fusion | flops 3221454848 | bytes 16777216 | tf_op jit(solution)/shard_map/pxyz,yk->pxkz/dot_general | solution.py:74
  225.1 88.9 %all-to-all-done = f32[128,16,8,128]{0,2,1,3:T(8,128)} async-done(((f32[128,16,8,128]{0,2,1,3:T(8,128)}), f32[128,16,8,128]{0,2,1,3:T(8,128)}, u32[]{:S(2)}, u32[]{:S(2)}) %all-to-all-start) | async-done | bytes 8388640 | tf_op jit(solution)/shard_map/all_to_all | solution.py:69
  314.0 11.5 %copy.97 = f32[128,16,16,8,8]{0,4,3,2,1:T(8,128)} copy(f32[128,16,16,8,8]{0,3,1,4,2:T(8,128)} %bitcast.6) | data formatting | bytes 16777216 | tf_op jit(solution)/shard_map/all_to_all | solution.py:69
  325.4 9.3 %copy.98 = f32[128,16,128,8]{2,0,3,1:T(8,128)} copy(f32[128,16,128,8]{0,3,2,1:T(8,128)} %bitcast.94) | data formatting | bytes 16777216 | tf_op jit(solution)/shard_map/all_to_all | solution.py:69
  334.7 12.4 %subtract_bitcast_fusion = f32[128,16,128,8]{0,2,3,1:T(8,128)S(1)} fusion(f32[128,128,16,8]{1,0,3,2:T(8,128)} %fusion.31, f32[128,16,128,8]{2,0,3,1:T(8,128)} %copy.98), kind=kOutput, calls=%fused_computation.7 | convolution fusion | flops 3223552000 | bytes 25165824 | tf_op jit(solution)/shard_map/pxyz,yk->pxkz/dot_general | solution.py:74
  347.2 8.1 %copy.111 = f32[128,16,128,8]{0,3,1,2:T(8,128)} copy(f32[128,16,128,8]{0,2,3,1:T(8,128)S(1)} %subtract_bitcast_fusion) | data formatting | bytes 16777216 | tf_op jit(solution)/shard_map/sub | solution.py:74
  355.2 5.6 all-to-all-start.3
  360.8 10.0 %fusion.33 = f32[128,128,16,8]{1,0,3,2:T(8,128)S(1)} fusion(f32[128,16,128,8]{2,0,3,1:T(8,128)} %copy.98), kind=kOutput, calls=%fused_computation.52 | convolution fusion | flops 3221454848 | bytes 16777216 | tf_op jit(solution)/shard_map/pxyz,yk->pxkz/dot_general | solution.py:71
  370.8 10.3 %add_bitcast_fusion = f32[128,16,128,8]{0,2,3,1:T(8,128)S(1)} fusion(f32[128,128,16,8]{1,0,3,2:T(8,128)S(1)} %fusion.33, f32[128,16,128,8]{2,0,3,1:T(8,128)} %copy.104), kind=kOutput, calls=%fused_computation.8 | convolution fusion | flops 3223552000 | bytes 25165824 | tf_op jit(solution)/shard_map/pxyz,yk->pxkz/dot_general | solution.py:71
  381.2 8.1 %copy.105 = f32[128,16,128,8]{0,3,1,2:T(8,128)} copy(f32[128,16,128,8]{0,2,3,1:T(8,128)S(1)} %add_bitcast_fusion) | data formatting | bytes 16777216 | tf_op jit(solution)/shard_map/add | solution.py:71
  389.2 66.2 %all-to-all-done.3 = f32[128,16,128,8]{0,3,1,2:T(8,128)} async-done(((f32[128,16,128,8]{0,3,1,2:T(8,128)}), f32[128,16,128,8]{0,3,1,2:T(8,128)}, u32[]{:S(2)}, u32[]{:S(2)}) %all-to-all-start.3) | async-done | bytes 8388640 | tf_op jit(solution)/shard_map/all_to_all | solution.py:80
  455.5 4.9 all-to-all-start.2
  460.5 0.8 and_select_fusion
  461.3 0.8 compare_and_fusion
  462.3 7.8 %copy.113 = f32[128,8,16,16,8]{0,4,3,2,1:T(8,128)} copy(f32[128,8,16,16,8]{0,4,2,3,1:T(8,128)} %bitcast.26) | data formatting | bytes 16777216 | tf_op jit(solution)/shard_map/all_to_all | solution.py:80
  470.1 9.3 %copy.114 = f32[128,128,128]{1,0,2:T(8,128)} copy(f32[128,128,128]{0,2,1:T(8,128)} %bitcast.95) | data formatting | bytes 16777216 | tf_op jit(solution)/shard_map/reshape | solution.py:34
  479.4 75.7 %all-to-all-done.2 = f32[128,16,128,8]{0,3,1,2:T(8,128)} async-done(((f32[128,16,128,8]{0,3,1,2:T(8,128)}), f32[128,16,128,8]{0,3,1,2:T(8,128)}, u32[]{:S(2)}, u32[]{:S(2)}) %all-to-all-start.2) | async-done | bytes 8388640 | tf_op jit(solution)/shard_map/all_to_all | solution.py:79
  555.0 7.8 %copy.107 = f32[128,8,16,16,8]{0,4,3,2,1:T(8,128)} copy(f32[128,8,16,16,8]{0,4,2,3,1:T(8,128)} %bitcast.18) | data formatting | bytes 16777216 | tf_op jit(solution)/shard_map/all_to_all | solution.py:79
  562.8 9.3 %copy.108 = f32[128,128,128]{1,0,2:T(8,128)} copy(f32[128,128,128]{0,2,1:T(8,128)} %bitcast.96) | data formatting | bytes 16777216 | tf_op jit(solution)/shard_map/reshape | solution.py:33
  572.2 6.2 gather_fusion.3
  578.4 6.2 gather_fusion.2
  584.5 4.9 fusion.5
  589.5 23.1 %all_gather.18 = f32[128,1024]{0,1:T(8,128)S(1)} all-gather(f32[128,64]{0,1:T(8,128)S(1)} %broadcast_multiply_fusion.1), channel_id=1, replica_groups=mesh['row'=8,'col'=16] {'col'}, dimensions={1}, use_global_device_ids=true | all-gather | bytes 557056 | tf_op jit(solution)/shard_map/all_gather | solution.py:89
  612.6 0.7 dynamic-slice_select_fusion.1
  613.4 22.3 %all_gather.21 = f32[128,1024]{0,1:T(8,128)S(1)} all-gather(f32[128,64]{0,1:T(8,128)S(1)} %broadcast_multiply_fusion), channel_id=1, replica_groups=mesh['row'=8,'col'=16] {'col'}, dimensions={1}, use_global_device_ids=true | all-gather | bytes 557056 | tf_op jit(solution)/shard_map/all_gather | solution.py:90
  635.7 0.7 dynamic-slice_select_fusion
  636.6 1.1 all-gather.5.cloned.1.call-done
  637.7 2.1 copy.128
  640.3 3.1 fusion.13
  643.4 1.8 fusion.17
  645.2 22.5 %all-gather.7.cloned.1.call-done = f32[1024,512]{0,1:T(8,128)} async-done(((f32[128,512]{0,1:T(8,128)}), f32[1024,512]{0,1:T(8,128)}) %all-gather.7.cloned.1.call-update) | async-done | bytes 2097168 | tf_op jit(solution)/shard_map/all_gather | solution.py:14
  667.7 2.2 copy.129
  670.5 4.1 fusion.10
  674.6 2.0 fusion.12
  676.6 2.5 pad_maximum_fusion
  (27 shorter events, 2.8 us)
Async XLA Ops:
  27.4 3.2 copy-start
  54.9 131.5 %all-to-all-start.1 = ((f32[128,16,8,128]{0,2,1,3:T(8,128)}), f32[128,16,8,128]{0,2,1,3:T(8,128)}, u32[]{:S(2)}, u32[]{:S(2)}) async-start(f32[128,16,8,128]{0,2,1,3:T(8,128)} %copy.101), calls=%async_computation.1 | async-start | bytes 16777216 | tf_op jit(solution)/shard_map/all_to_all | solution.py:70
  186.3 127.6 %all-to-all-start = ((f32[128,16,8,128]{0,2,1,3:T(8,128)}), f32[128,16,8,128]{0,2,1,3:T(8,128)}, u32[]{:S(2)}, u32[]{:S(2)}) async-start(f32[128,16,8,128]{0,2,1,3:T(8,128)} %copy.95), calls=%async_computation | async-start | bytes 16777216 | tf_op jit(solution)/shard_map/all_to_all | solution.py:69
  355.2 100.2 %all-to-all-start.3 = ((f32[128,16,128,8]{0,3,1,2:T(8,128)}), f32[128,16,128,8]{0,3,1,2:T(8,128)}, u32[]{:S(2)}, u32[]{:S(2)}) async-start(f32[128,16,128,8]{0,3,1,2:T(8,128)} %copy.111), calls=%async_computation.3 | async-start | bytes 16777216 | tf_op jit(solution)/shard_map/all_to_all | solution.py:80
  455.5 99.6 %all-to-all-start.2 = ((f32[128,16,128,8]{0,3,1,2:T(8,128)}), f32[128,16,128,8]{0,3,1,2:T(8,128)}, u32[]{:S(2)}, u32[]{:S(2)}) async-start(f32[128,16,128,8]{0,3,1,2:T(8,128)} %copy.105), calls=%async_computation.2 | async-start | bytes 16777216 | tf_op jit(solution)/shard_map/all_to_all | solution.py:79
  460.4 177.3 %all-gather.5.cloned.1.call-start = ((), (), s32[]{:S(2)}) async-start(), calls=%async_computation.4 | async-start | bytes 2359296 | tf_op jit(solution)/shard_map/all_gather | solution.py:14
  584.5 51.9 %copy-start.2 = (s32[128]{0:T(128)S(1)}, s32[128]{0:T(128)}, u32[]{:S(2)}) copy-start(s32[128]{0:T(128)} %param.17) | copy-start | bytes 1540
  584.5 51.9 %copy-start.3 = (s32[128]{0:T(128)S(1)}, s32[128]{0:T(128)}, u32[]{:S(2)}) copy-start(s32[128]{0:T(128)} %param.16) | copy-start | bytes 1540
  584.5 52.0 %copy-start.4 = (f32[64]{0:T(128)S(1)}, f32[64]{0:T(128)}, u32[]{:S(2)}) copy-start(f32[64]{0:T(128)} %param.14) | copy-start | bytes 772
  584.5 52.0 %copy-start.5 = (f32[64]{0:T(128)S(1)}, f32[64]{0:T(128)}, u32[]{:S(2)}) copy-start(f32[64]{0:T(128)} %param.15) | copy-start | bytes 772
  613.4 54.4 %all-gather.7.cloned.1.call-start = ((), (), s32[]{:S(2)}) async-start(), calls=%async_computation.5 | async-start | bytes 2359296 | tf_op jit(solution)/shard_map/all_gather | solution.py:14
  667.7 6.9 copy-start.1
Sparse Core Ops, SparseCore 0:
  613.5 24.1 all-gather.4
  639.4 28.2 all-gather.6
